TPU v7x, 512 devices: a whole 4x4x16 slice. The times are simulated.
512 devices in a mesh: row: 32 (over z, core), band: 16 (over y, x).
Axes of the slice: x: 4, y: 4, z: 16, core: 2. Of those that a mesh axis runs over, the one named last changes fastest.
Arguments:
- band_blocks: bfloat16 [1024, 16, 128, 128], P('row', 'band'), may hold values from 0 to 0.006591797, as said below
- distant_block_slots: bfloat16 [32, 16, 32, 2, 128, 128], P('row', 'band'), may hold values from 0 to 0.00033203125, as said below
- far_rows: int32 [32, 16, 32, 2], P('row', 'band'), may hold values from 0 to 31
- far_columns: int32 [32, 16, 32, 2], P('row', 'band'), may hold values from 0 to 31
- far_counts: int32 [32, 16, 32], P('row', 'band'), may hold values from 0 to 2, as said below
Outputs:
- scaling: float32 [1024, 128], P('row')
- residual: float32 [1024, 128], P('row')
Inputs may be any that keep to these rules, and one draw needn't show every extreme that they name: `band_blocks`: positive entries; offset-0 blocks symmetric. `distant_block_slots`: positive entries. `far_counts`: some target range receives 2 live slots from every device.
All inputs are finite; a program needn't handle non-finite values.
Results may differ from a plain program's by a relative error of at most 0.0116.
The roundings to bfloat16 on the way count: a program that leaves them out, or rounds other values in their place, can miss the bound.
Values may be sent and summed in bfloat16 or wider, within the bound.
No kernel may reach another device: no remote copies, remote signals or barrier semaphores. Data moves between devices by JAX's collectives and lax.ppermute only.
A program may use at most 64 MiB of HBM per device.

v0:
```python
import jax
import jax.numpy as jnp
from jax import lax
from jax.sharding import PartitionSpec as P

OUTER = 2
INNER = 2


def shifted(value, axis, steps):
    count = lax.axis_size(axis)
    leading, last = (max(0, -steps), min(count, count - steps))
    return lax.ppermute(value, axis, [(source, source + steps) for source in range(leading, last)])


def on_device(band_blocks, distant_block_slots, far_rows, far_columns, far_counts):
    rows_dev = band_blocks.shape[0]
    block_size = band_blocks.shape[2]
    band_count = lax.axis_size("band")
    row_count = lax.axis_size("row")
    offset = lax.axis_index("band")
    row_index = lax.axis_index("row")
    blocks = band_blocks[:, 0]
    distant_local_part = distant_block_slots[0, 0]
    local_row_values = far_rows[0, 0]
    columns_local = far_columns[0, 0]
    counts = far_counts[0, 0]
    slots = local_row_values.shape[1]
    live_mask = (jnp.arange(slots)[None, :] < counts[:, None]).astype(jnp.float32)[..., None]
    block_ids = row_index * rows_dev + jnp.arange(rows_dev)
    valid_mask = (block_ids + offset < row_count * rows_dev).astype(jnp.float32)[:, None]
    upper_mask = (offset > 0).astype(jnp.float32)
    wanted = lax.all_to_all(columns_local, "row", split_axis=0, concat_axis=0, tiled=True)
    targets = jnp.arange(rows_dev)[None, :]
    selection_output = (wanted.reshape(-1)[:, None] == targets).astype(jnp.float32)
    pick_in = (local_row_values.reshape(-1)[:, None] == targets).astype(jnp.float32)

    def multiply(vector):
        narrow_band_part = vector.astype(jnp.bfloat16)
        ahead_rows = shifted(narrow_band_part[:band_count], "row", -1)
        extended = jnp.concatenate([narrow_band_part, ahead_rows], 0)
        columns = lax.dynamic_slice_in_dim(extended, offset, rows_dev, 0)
        forward = (
            jnp.einsum("kij,kj->ki", blocks, columns, preferred_element_type=jnp.float32)
            * valid_mask
        )
        backward = jnp.einsum(
            "kij,ki->kj", blocks, narrow_band_part, preferred_element_type=jnp.float32
        ) * (valid_mask * upper_mask)
        spread = lax.dynamic_update_slice_in_dim(
            jnp.zeros((rows_dev + band_count, block_size), jnp.float32), backward, offset, 0
        )
        outgoing = narrow_band_part[wanted]
        gathered_values = lax.all_to_all(outgoing, "row", split_axis=0, concat_axis=0, tiled=True)
        far_forward = (
            jnp.einsum(
                "oqht,oqt->oqh",
                distant_local_part,
                gathered_values,
                preferred_element_type=jnp.float32,
            )
            * live_mask
        )
        far_backward = (
            jnp.einsum(
                "nquo,nqu->nqo",
                distant_local_part,
                narrow_band_part[local_row_values],
                preferred_element_type=jnp.float32,
            )
            * live_mask
        )
        returned = lax.all_to_all(far_backward, "row", split_axis=0, concat_axis=0, tiled=True)
        summed = forward + spread[:rows_dev]
        summed = summed + jnp.dot(
            pick_in.T, far_forward.reshape(-1, block_size), precision=lax.Precision.HIGHEST
        )
        summed = summed + jnp.dot(
            selection_output.T, returned.reshape(-1, block_size), precision=lax.Precision.HIGHEST
        )
        carried = shifted(spread[rows_dev:], "row", 1)
        summed = jnp.concatenate([summed[:band_count] + carried, summed[band_count:]], 0)
        return lax.psum(summed, "band")

    row_sums = multiply(jnp.ones((rows_dev, block_size), jnp.float32))
    scaling = 1.0 / jnp.sqrt(row_sums)
    residual = jnp.zeros_like(scaling)
    for outer_step in range(OUTER):
        balance = scaling * multiply(scaling)
        residual = 1.0 - balance
        scaled = residual / balance
        direction = scaled
        current_residual_product = lax.psum(jnp.sum(residual * scaled), "row")
        growth = jnp.ones_like(scaling)
        for inner_step in range(INNER):
            curved = scaling * multiply(scaling * direction) + balance * direction
            curvature = lax.psum(jnp.sum(direction * curved), "row")
            step_size = current_residual_product / curvature
            growth = growth + step_size * direction
            residual = residual - step_size * curved
            if inner_step + 1 < INNER:
                scaled = residual / balance
                rho_next = lax.psum(jnp.sum(residual * scaled), "row")
                direction = scaled + rho_next / current_residual_product * direction
                current_residual_product = rho_next
        scaling = scaling * growth
    return (scaling, residual)


def solution(mesh):
    return jax.shard_map(
        on_device,
        mesh=mesh,
        in_specs=(
            P("row", "band", None, None),
            P("row", "band", None, None, None, None),
            P("row", "band", None, None),
            P("row", "band", None, None),
            P("row", "band", None),
        ),
        out_specs=(P("row", None), P("row", None)),
        check_vma=False,
    )
```

profile of v0, /device:TPU:1, one launch (start us, length us, event | category | flops | bytes accessed | tf_op | source)
XLA Modules:
  0.0 1086.6 jit_solution(9231055719620302037)
XLA Ops:
  0.7 9.0 collective-permute-start
  9.7 1.4 copy.16
  11.1 10.0 all-to-all-start
  21.1 1.6 fusion.52
  23.0 3.5 collective-permute-start.1
  28.1 4.7 all-to-all-done
  33.8 1.2 gather_fusion
  35.0 6.2 all-to-all-start.1
  44.7 8.2 all-to-all-done.1
  54.8 4.4 all-to-all-start.2
  59.5 12.0 %all-to-all-done.2 = f32[32,2,128]{2,1,0:T(2,128)S(1)} async-done(((f32[32,2,128]{2,1,0:T(2,128)}), f32[32,2,128]{2,1,0:T(2,128)S(1)}, u32[]{:S(2)}, u32[]{:S(2)}) %all-to-all-start.2) | async-done | bytes 32800 | tf_op jit(solution)/shard_map/all_to_all | solution.py:73
  71.8 60.6 %psum.105 = f32[32,128]{1,0:T(8,128)S(1)} all-reduce(f32[32,128]{1,0:T(8,128)S(1)} %pad_maximum_fusion), channel_id=1, replica_groups=mesh['row'=32,'band'=16] {'band'}, use_global_device_ids=true, to_apply=%region_0.0 | all-reduce | flops 4096 | bytes 32768 | tf_op jit(solution)/shard_map/psum | solution.py:83
  132.4 1.2 gather_fusion.2
  134.3 16.9 %collective-permute-start.2 = (bf16[16,128]{1,0:T(8,128)(2,1)S(1)}, bf16[16,128]{1,0:T(8,128)(2,1)S(1)}, u32[]{:S(2)}, u32[]{:S(2)}) collective-permute-start(bf16[16,128]{1,0:T(8,128)(2,1)S(1)} %slice.172), channel_id=1, source_target_pairs={{16,0},{32,16},{48,32},{64,48},{80,64},{96,80},{112,96},{128,112},... | collective-permute-start | bytes 12296 | tf_op jit(solution)/shard_map/ppermute | solution.py:13
  151.2 3.6 all-to-all-start.3
  156.2 2.8 collective-permute-start.3
  159.7 6.2 all-to-all-done.3
  167.8 4.7 all-to-all-start.4
  172.8 11.8 %all-to-all-done.4 = f32[32,2,128]{2,1,0:T(2,128)S(1)} async-done(((f32[32,2,128]{2,1,0:T(2,128)}), f32[32,2,128]{2,1,0:T(2,128)S(1)}, u32[]{:S(2)}, u32[]{:S(2)}) %all-to-all-start.4) | async-done | bytes 32800 | tf_op jit(solution)/shard_map/all_to_all | solution.py:73
  184.9 55.9 %psum.106 = f32[32,128]{1,0:T(8,128)S(1)} all-reduce(f32[32,128]{1,0:T(8,128)S(1)} %pad_maximum_fusion.1), channel_id=1, replica_groups=mesh['row'=32,'band'=16] {'band'}, use_global_device_ids=true, to_apply=%region_1.0 | all-reduce | flops 4096 | bytes 32768 | tf_op jit(solution)/shard_map/psum | solution.py:83
  240.8 1.2 gather_fusion.4
  242.7 16.7 %collective-permute-start.4 = (bf16[16,128]{1,0:T(8,128)(2,1)S(1)}, bf16[16,128]{1,0:T(8,128)(2,1)S(1)}, u32[]{:S(2)}, u32[]{:S(2)}) collective-permute-start(bf16[16,128]{1,0:T(8,128)(2,1)S(1)} %slice.177), channel_id=1, source_target_pairs={{16,0},{32,16},{48,32},{64,48},{80,64},{96,80},{112,96},{128,112},... | collective-permute-start | bytes 12296 | tf_op jit(solution)/shard_map/ppermute | solution.py:13
  259.4 3.6 all-to-all-start.5
  264.4 2.8 collective-permute-start.5
  267.9 6.2 all-to-all-done.5
  276.0 4.7 all-to-all-start.6
  281.0 11.8 %all-to-all-done.6 = f32[32,2,128]{2,1,0:T(2,128)S(1)} async-done(((f32[32,2,128]{2,1,0:T(2,128)}), f32[32,2,128]{2,1,0:T(2,128)S(1)}, u32[]{:S(2)}, u32[]{:S(2)}) %all-to-all-start.6) | async-done | bytes 32800 | tf_op jit(solution)/shard_map/all_to_all | solution.py:73
  293.1 55.9 %psum.108 = f32[32,128]{1,0:T(8,128)S(1)} all-reduce(f32[32,128]{1,0:T(8,128)S(1)} %pad_maximum_fusion.2), channel_id=1, replica_groups=mesh['row'=32,'band'=16] {'band'}, use_global_device_ids=true, to_apply=%region_4.0 | all-reduce | flops 4096 | bytes 32768 | tf_op jit(solution)/shard_map/psum | solution.py:83
  349.6 60.6 %all-reduce.2 = (f32[]{:T(128)}, f32[]{:T(128)}) all-reduce(f32[]{:T(128)} %get-tuple-element.3, f32[]{:T(128)} %get-tuple-element.2), channel_id=1, replica_groups=mesh['row'=32,'band'=16] {'row'}, use_global_device_ids=true, to_apply=%region_3.0 | all-reduce | flops 2 | bytes 16 | tf_op jit(solution)/shard_map/psum | solution.py:93
  412.1 46.4 %psum.110 = f32[]{:T(128)} all-reduce(f32[]{:T(128)} %multiply_reduce_fusion.4), channel_id=1, replica_groups=mesh['row'=32,'band'=16] {'row'}, use_global_device_ids=true, to_apply=%region_8.0 | all-reduce | flops 1 | bytes 8 | tf_op jit(solution)/shard_map/psum | solution.py:103
  459.8 1.2 gather_fusion.6
  461.7 2.5 collective-permute-start.6
  464.3 3.8 all-to-all-start.7
  469.4 3.0 collective-permute-start.7
  473.1 6.0 all-to-all-done.7
  481.0 4.8 all-to-all-start.8
  486.0 11.8 %all-to-all-done.8 = f32[32,2,128]{2,1,0:T(2,128)S(1)} async-done(((f32[32,2,128]{2,1,0:T(2,128)}), f32[32,2,128]{2,1,0:T(2,128)S(1)}, u32[]{:S(2)}, u32[]{:S(2)}) %all-to-all-start.8) | async-done | bytes 32800 | tf_op jit(solution)/shard_map/all_to_all | solution.py:73
  498.1 55.9 %psum.111 = f32[32,128]{1,0:T(8,128)S(1)} all-reduce(f32[32,128]{1,0:T(8,128)S(1)} %pad_maximum_fusion.3), channel_id=1, replica_groups=mesh['row'=32,'band'=16] {'band'}, use_global_device_ids=true, to_apply=%region_9.0 | all-reduce | flops 4096 | bytes 32768 | tf_op jit(solution)/shard_map/psum | solution.py:83
  554.6 60.6 %psum.112 = f32[]{:T(128)} all-reduce(f32[]{:T(128)} %multiply_reduce_fusion.3), channel_id=1, replica_groups=mesh['row'=32,'band'=16] {'row'}, use_global_device_ids=true, to_apply=%region_11.0 | all-reduce | flops 1 | bytes 8 | tf_op jit(solution)/shard_map/psum | solution.py:97
  616.5 1.2 gather_fusion.8
  618.4 2.5 collective-permute-start.8
  620.9 3.6 all-to-all-start.9
  625.9 3.0 collective-permute-start.9
  629.6 6.0 all-to-all-done.9
  637.5 4.8 all-to-all-start.10
  642.5 11.8 %all-to-all-done.10 = f32[32,2,128]{2,1,0:T(2,128)S(1)} async-done(((f32[32,2,128]{2,1,0:T(2,128)}), f32[32,2,128]{2,1,0:T(2,128)S(1)}, u32[]{:S(2)}, u32[]{:S(2)}) %all-to-all-start.10) | async-done | bytes 32800 | tf_op jit(solution)/shard_map/all_to_all | solution.py:73
  654.6 55.9 %psum.113 = f32[32,128]{1,0:T(8,128)S(1)} all-reduce(f32[32,128]{1,0:T(8,128)S(1)} %pad_maximum_fusion.4), channel_id=1, replica_groups=mesh['row'=32,'band'=16] {'band'}, use_global_device_ids=true, to_apply=%region_12.0 | all-reduce | flops 4096 | bytes 32768 | tf_op jit(solution)/shard_map/psum | solution.py:83
  712.4 16.7 %collective-permute-start.10 = (bf16[16,128]{1,0:T(8,128)(2,1)S(1)}, bf16[16,128]{1,0:T(8,128)(2,1)S(1)}, u32[]{:S(2)}, u32[]{:S(2)}) collective-permute-start(bf16[16,128]{1,0:T(8,128)(2,1)S(1)} %slice.192), channel_id=1, source_target_pairs={{16,0},{32,16},{48,32},{64,48},{80,64},{96,80},{112,96},{128,112},... | collective-permute-start | bytes 12296 | tf_op jit(solution)/shard_map/ppermute | solution.py:13
  729.1 3.6 all-to-all-start.11
  734.1 2.8 collective-permute-start.11
  737.6 6.2 all-to-all-done.11
  745.7 4.7 all-to-all-start.12
  750.7 11.8 %all-to-all-done.12 = f32[32,2,128]{2,1,0:T(2,128)S(1)} async-done(((f32[32,2,128]{2,1,0:T(2,128)}), f32[32,2,128]{2,1,0:T(2,128)S(1)}, u32[]{:S(2)}, u32[]{:S(2)}) %all-to-all-start.12) | async-done | bytes 32800 | tf_op jit(solution)/shard_map/all_to_all | solution.py:73
  762.8 55.9 %psum.115 = f32[32,128]{1,0:T(8,128)S(1)} all-reduce(f32[32,128]{1,0:T(8,128)S(1)} %pad_maximum_fusion.5), channel_id=1, replica_groups=mesh['row'=32,'band'=16] {'band'}, use_global_device_ids=true, to_apply=%region_15.0 | all-reduce | flops 4096 | bytes 32768 | tf_op jit(solution)/shard_map/psum | solution.py:83
  819.3 60.6 %all-reduce.1 = (f32[]{:T(128)}, f32[]{:T(128)}) all-reduce(f32[]{:T(128)} %get-tuple-element.5, f32[]{:T(128)} %get-tuple-element.4), channel_id=1, replica_groups=mesh['row'=32,'band'=16] {'row'}, use_global_device_ids=true, to_apply=%region_14.0 | all-reduce | flops 2 | bytes 16 | tf_op jit(solution)/shard_map/psum | solution.py:93
  881.9 46.4 %psum.117 = f32[]{:T(128)} all-reduce(f32[]{:T(128)} %get-tuple-element.10), channel_id=1, replica_groups=mesh['row'=32,'band'=16] {'row'}, use_global_device_ids=true, to_apply=%region_19.0 | all-reduce | flops 1 | bytes 8 | tf_op jit(solution)/shard_map/psum | solution.py:103
  931.4 2.5 collective-permute-start.12
  934.0 3.6 all-to-all-start.13
  938.9 3.0 collective-permute-start.13
  942.7 6.0 all-to-all-done.13
  950.5 4.8 all-to-all-start.14
  955.6 11.8 %all-to-all-done.14 = f32[32,2,128]{2,1,0:T(2,128)S(1)} async-done(((f32[32,2,128]{2,1,0:T(2,128)}), f32[32,2,128]{2,1,0:T(2,128)S(1)}, u32[]{:S(2)}, u32[]{:S(2)}) %all-to-all-start.14) | async-done | bytes 32800 | tf_op jit(solution)/shard_map/all_to_all | solution.py:73
  967.7 55.9 %psum.118 = f32[32,128]{1,0:T(8,128)S(1)} all-reduce(f32[32,128]{1,0:T(8,128)S(1)} %pad_maximum_fusion.6), channel_id=1, replica_groups=mesh['row'=32,'band'=16] {'band'}, use_global_device_ids=true, to_apply=%region_20.0 | all-reduce | flops 4096 | bytes 32768 | tf_op jit(solution)/shard_map/psum | solution.py:83
  1024.2 60.6 %psum.119 = f32[]{:T(128)} all-reduce(f32[]{:T(128)} %multiply_reduce_fusion), channel_id=1, replica_groups=mesh['row'=32,'band'=16] {'row'}, use_global_device_ids=true, to_apply=%region_22.0 | all-reduce | flops 1 | bytes 8 | tf_op jit(solution)/shard_map/psum | solution.py:97
  (162 shorter events, 46.1 us)
Async XLA Ops:
  0.6 41.4 %copy-start = (bf16[1,1,32,2,128,128]{5,4,3,2,1,0:T(8,128)(2,1)S(1)}, bf16[1,1,32,2,128,128]{5,4,3,2,1,0:T(8,128)(2,1)}, u32[]{:S(2)}) copy-start(bf16[1,1,32,2,128,128]{5,4,3,2,1,0:T(8,128)(2,1)} %param.6) | copy-start | bytes 6291460
  0.6 43.4 %copy-start.1 = (bf16[32,1,128,128]{3,2,1,0:T(8,128)(2,1)S(1)}, bf16[32,1,128,128]{3,2,1,0:T(8,128)(2,1)}, u32[]{:S(2)}) copy-start(bf16[32,1,128,128]{3,2,1,0:T(8,128)(2,1)} %param.5) | copy-start | bytes 3145732
  0.7 43.3 %collective-permute-start = (bf16[16,128]{1,0:T(8,128)(2,1)S(1)}, bf16[16,128]{1,0:T(8,128)(2,1)S(1)}, u32[]{:S(2)}, u32[]{:S(2)}) collective-permute-start(bf16[16,128]{1,0:T(8,128)(2,1)S(1)} %slice.105), channel_id=1, source_target_pairs={{16,0},{32,16},{48,32},{64,48},{80,64},{96,80},{112,96},{128,112},... | collective-permute-start | bytes 12296 | tf_op jit(solution)/shard_map/ppermute | solution.py:13
  11.1 21.8 %all-to-all-start = ((s32[32,1,2]{2,1,0:T(1,128)}), s32[32,1,2]{2,1,0:T(1,128)S(1)}, u32[]{:S(2)}, u32[]{:S(2)}) async-start(s32[32,1,2]{2,1,0:T(1,128)} %copy.16), calls=%async_computation | async-start | bytes 32768 | tf_op jit(solution)/shard_map/all_to_all | solution.py:33
  23.0 48.8 %collective-permute-start.1 = (f32[16,128]{1,0:T(8,128)S(1)}, f32[16,128]{1,0:T(8,128)S(1)}, u32[]{:S(2)}, u32[]{:S(2)}) collective-permute-start(f32[16,128]{1,0:T(8,128)S(1)} %slice.170), channel_id=1, source_target_pairs={{0,16},{16,32},{32,48},{48,64},{64,80},{80,96},{96,112},{112,128},... | collective-permute-start | bytes 24584 | tf_op jit(solution)/shard_map/ppermute | solution.py:13
  35.0 17.9 %all-to-all-start.1 = ((bf16[32,2,128]{2,1,0:T(2,128)(2,1)}), bf16[32,2,128]{2,1,0:T(2,128)(2,1)S(1)}, u32[]{:S(2)}, u32[]{:S(2)}) async-start(bf16[32,2,128]{2,1,0:T(2,128)(2,1)} %bitcast.8), calls=%async_computation.1 | async-start | bytes 32768 | tf_op jit(solution)/shard_map/all_to_all | solution.py:54
  54.8 16.6 %all-to-all-start.2 = ((f32[32,2,128]{2,1,0:T(2,128)}), f32[32,2,128]{2,1,0:T(2,128)S(1)}, u32[]{:S(2)}, u32[]{:S(2)}) async-start(f32[32,2,128]{2,1,0:T(2,128)} %get-tuple-element.45), calls=%async_computation.2 | async-start | bytes 65536 | tf_op jit(solution)/shard_map/all_to_all | solution.py:73
  134.3 24.7 %collective-permute-start.2 = (bf16[16,128]{1,0:T(8,128)(2,1)S(1)}, bf16[16,128]{1,0:T(8,128)(2,1)S(1)}, u32[]{:S(2)}, u32[]{:S(2)}) collective-permute-start(bf16[16,128]{1,0:T(8,128)(2,1)S(1)} %slice.172), channel_id=1, source_target_pairs={{16,0},{32,16},{48,32},{64,48},{80,64},{96,80},{112,96},{128,112},... | collective-permute-start | bytes 12296 | tf_op jit(solution)/shard_map/ppermute | solution.py:13
  151.2 14.7 %all-to-all-start.3 = ((bf16[32,2,128]{2,1,0:T(2,128)(2,1)}), bf16[32,2,128]{2,1,0:T(2,128)(2,1)S(1)}, u32[]{:S(2)}, u32[]{:S(2)}) async-start(bf16[32,2,128]{2,1,0:T(2,128)(2,1)} %bitcast.27), calls=%async_computation.3 | async-start | bytes 32768 | tf_op jit(solution)/shard_map/all_to_all | solution.py:54
  156.2 28.7 %collective-permute-start.3 = (f32[16,128]{1,0:T(8,128)S(1)}, f32[16,128]{1,0:T(8,128)S(1)}, u32[]{:S(2)}, u32[]{:S(2)}) collective-permute-start(f32[16,128]{1,0:T(8,128)S(1)} %slice.175), channel_id=1, source_target_pairs={{0,16},{16,32},{32,48},{48,64},{64,80},{80,96},{96,112},{112,128},... | collective-permute-start | bytes 24584 | tf_op jit(solution)/shard_map/ppermute | solution.py:13
  167.8 16.8 %all-to-all-start.4 = ((f32[32,2,128]{2,1,0:T(2,128)}), f32[32,2,128]{2,1,0:T(2,128)S(1)}, u32[]{:S(2)}, u32[]{:S(2)}) async-start(f32[32,2,128]{2,1,0:T(2,128)} %get-tuple-element.41), calls=%async_computation.4 | async-start | bytes 65536 | tf_op jit(solution)/shard_map/all_to_all | solution.py:73
  242.7 24.5 %collective-permute-start.4 = (bf16[16,128]{1,0:T(8,128)(2,1)S(1)}, bf16[16,128]{1,0:T(8,128)(2,1)S(1)}, u32[]{:S(2)}, u32[]{:S(2)}) collective-permute-start(bf16[16,128]{1,0:T(8,128)(2,1)S(1)} %slice.177), channel_id=1, source_target_pairs={{16,0},{32,16},{48,32},{64,48},{80,64},{96,80},{112,96},{128,112},... | collective-permute-start | bytes 12296 | tf_op jit(solution)/shard_map/ppermute | solution.py:13
  259.4 14.7 %all-to-all-start.5 = ((bf16[32,2,128]{2,1,0:T(2,128)(2,1)}), bf16[32,2,128]{2,1,0:T(2,128)(2,1)S(1)}, u32[]{:S(2)}, u32[]{:S(2)}) async-start(bf16[32,2,128]{2,1,0:T(2,128)(2,1)} %bitcast.43), calls=%async_computation.5 | async-start | bytes 32768 | tf_op jit(solution)/shard_map/all_to_all | solution.py:54
  264.4 28.7 %collective-permute-start.5 = (f32[16,128]{1,0:T(8,128)S(1)}, f32[16,128]{1,0:T(8,128)S(1)}, u32[]{:S(2)}, u32[]{:S(2)}) collective-permute-start(f32[16,128]{1,0:T(8,128)S(1)} %slice.180), channel_id=1, source_target_pairs={{0,16},{16,32},{32,48},{48,64},{64,80},{80,96},{96,112},{112,128},... | collective-permute-start | bytes 24584 | tf_op jit(solution)/shard_map/ppermute | solution.py:13
  276.0 16.8 %all-to-all-start.6 = ((f32[32,2,128]{2,1,0:T(2,128)}), f32[32,2,128]{2,1,0:T(2,128)S(1)}, u32[]{:S(2)}, u32[]{:S(2)}) async-start(f32[32,2,128]{2,1,0:T(2,128)} %get-tuple-element.37), calls=%async_computation.6 | async-start | bytes 65536 | tf_op jit(solution)/shard_map/all_to_all | solution.py:73
  461.7 10.7 collective-permute-start.6
  464.3 14.8 %all-to-all-start.7 = ((bf16[32,2,128]{2,1,0:T(2,128)(2,1)}), bf16[32,2,128]{2,1,0:T(2,128)(2,1)S(1)}, u32[]{:S(2)}, u32[]{:S(2)}) async-start(bf16[32,2,128]{2,1,0:T(2,128)(2,1)} %bitcast.59), calls=%async_computation.7 | async-start | bytes 32768 | tf_op jit(solution)/shard_map/all_to_all | solution.py:54
  469.4 28.7 %collective-permute-start.7 = (f32[16,128]{1,0:T(8,128)S(1)}, f32[16,128]{1,0:T(8,128)S(1)}, u32[]{:S(2)}, u32[]{:S(2)}) collective-permute-start(f32[16,128]{1,0:T(8,128)S(1)} %slice.185), channel_id=1, source_target_pairs={{0,16},{16,32},{32,48},{48,64},{64,80},{80,96},{96,112},{112,128},... | collective-permute-start | bytes 24584 | tf_op jit(solution)/shard_map/ppermute | solution.py:13
  481.0 16.8 %all-to-all-start.8 = ((f32[32,2,128]{2,1,0:T(2,128)}), f32[32,2,128]{2,1,0:T(2,128)S(1)}, u32[]{:S(2)}, u32[]{:S(2)}) async-start(f32[32,2,128]{2,1,0:T(2,128)} %get-tuple-element.33), calls=%async_computation.8 | async-start | bytes 65536 | tf_op jit(solution)/shard_map/all_to_all | solution.py:73
  618.4 10.5 collective-permute-start.8
  620.9 14.7 %all-to-all-start.9 = ((bf16[32,2,128]{2,1,0:T(2,128)(2,1)}), bf16[32,2,128]{2,1,0:T(2,128)(2,1)S(1)}, u32[]{:S(2)}, u32[]{:S(2)}) async-start(bf16[32,2,128]{2,1,0:T(2,128)(2,1)} %bitcast.75), calls=%async_computation.9 | async-start | bytes 32768 | tf_op jit(solution)/shard_map/all_to_all | solution.py:54
  625.9 28.7 %collective-permute-start.9 = (f32[16,128]{1,0:T(8,128)S(1)}, f32[16,128]{1,0:T(8,128)S(1)}, u32[]{:S(2)}, u32[]{:S(2)}) collective-permute-start(f32[16,128]{1,0:T(8,128)S(1)} %slice.190), channel_id=1, source_target_pairs={{0,16},{16,32},{32,48},{48,64},{64,80},{80,96},{96,112},{112,128},... | collective-permute-start | bytes 24584 | tf_op jit(solution)/shard_map/ppermute | solution.py:13
  637.5 16.8 %all-to-all-start.10 = ((f32[32,2,128]{2,1,0:T(2,128)}), f32[32,2,128]{2,1,0:T(2,128)S(1)}, u32[]{:S(2)}, u32[]{:S(2)}) async-start(f32[32,2,128]{2,1,0:T(2,128)} %get-tuple-element.29), calls=%async_computation.10 | async-start | bytes 65536 | tf_op jit(solution)/shard_map/all_to_all | solution.py:73
  712.4 24.5 %collective-permute-start.10 = (bf16[16,128]{1,0:T(8,128)(2,1)S(1)}, bf16[16,128]{1,0:T(8,128)(2,1)S(1)}, u32[]{:S(2)}, u32[]{:S(2)}) collective-permute-start(bf16[16,128]{1,0:T(8,128)(2,1)S(1)} %slice.192), channel_id=1, source_target_pairs={{16,0},{32,16},{48,32},{64,48},{80,64},{96,80},{112,96},{128,112},... | collective-permute-start | bytes 12296 | tf_op jit(solution)/shard_map/ppermute | solution.py:13
  729.1 14.7 %all-to-all-start.11 = ((bf16[32,2,128]{2,1,0:T(2,128)(2,1)}), bf16[32,2,128]{2,1,0:T(2,128)(2,1)S(1)}, u32[]{:S(2)}, u32[]{:S(2)}) async-start(bf16[32,2,128]{2,1,0:T(2,128)(2,1)} %bitcast.91), calls=%async_computation.11 | async-start | bytes 32768 | tf_op jit(solution)/shard_map/all_to_all | solution.py:54
  734.1 28.7 %collective-permute-start.11 = (f32[16,128]{1,0:T(8,128)S(1)}, f32[16,128]{1,0:T(8,128)S(1)}, u32[]{:S(2)}, u32[]{:S(2)}) collective-permute-start(f32[16,128]{1,0:T(8,128)S(1)} %slice.195), channel_id=1, source_target_pairs={{0,16},{16,32},{32,48},{48,64},{64,80},{80,96},{96,112},{112,128},... | collective-permute-start | bytes 24584 | tf_op jit(solution)/shard_map/ppermute | solution.py:13
  745.7 16.8 %all-to-all-start.12 = ((f32[32,2,128]{2,1,0:T(2,128)}), f32[32,2,128]{2,1,0:T(2,128)S(1)}, u32[]{:S(2)}, u32[]{:S(2)}) async-start(f32[32,2,128]{2,1,0:T(2,128)} %get-tuple-element.25), calls=%async_computation.12 | async-start | bytes 65536 | tf_op jit(solution)/shard_map/all_to_all | solution.py:73
  931.4 10.5 collective-permute-start.12
  934.0 14.7 %all-to-all-start.13 = ((bf16[32,2,128]{2,1,0:T(2,128)(2,1)}), bf16[32,2,128]{2,1,0:T(2,128)(2,1)S(1)}, u32[]{:S(2)}, u32[]{:S(2)}) async-start(bf16[32,2,128]{2,1,0:T(2,128)(2,1)} %bitcast.107), calls=%async_computation.13 | async-start | bytes 32768 | tf_op jit(solution)/shard_map/all_to_all | solution.py:54
  938.9 28.7 %collective-permute-start.13 = (f32[16,128]{1,0:T(8,128)S(1)}, f32[16,128]{1,0:T(8,128)S(1)}, u32[]{:S(2)}, u32[]{:S(2)}) collective-permute-start(f32[16,128]{1,0:T(8,128)S(1)} %slice.200), channel_id=1, source_target_pairs={{0,16},{16,32},{32,48},{48,64},{64,80},{80,96},{96,112},{112,128},... | collective-permute-start | bytes 24584 | tf_op jit(solution)/shard_map/ppermute | solution.py:13
  950.5 16.8 %all-to-all-start.14 = ((f32[32,2,128]{2,1,0:T(2,128)}), f32[32,2,128]{2,1,0:T(2,128)S(1)}, u32[]{:S(2)}, u32[]{:S(2)}) async-start(f32[32,2,128]{2,1,0:T(2,128)} %get-tuple-element.21), calls=%async_computation.14 | async-start | bytes 65536 | tf_op jit(solution)/shard_map/all_to_all | solution.py:73
where the time goes:
time: 1090 us
  blocking collectives  731 us (67%)
  starting transfers between devices  159 us (15%)
  waiting for transfers between devices  132 us (12%)
  matrix products  24.9 us (2%)
  local copies, waits for them, and re-layouts  17.9 us (2%)
  other arithmetic  12.5 us (1%)
    psum x7, blocking collectives, multiply(): return lax.psum(summed, 'band')  396 us
    psum x2, blocking collectives, on_device(): current_residual_product = lax.psum(jnp.sum(residual * scaled), 'row')  121 us
    psum x2, blocking collectives, on_device(): curvature = lax.psum(jnp.sum(direction * curved), 'row')  121 us
    psum x2, blocking collectives, on_device(): rho_next = lax.psum(jnp.sum(residual * scaled), 'row')  92.8 us
    ppermute x14, starting transfers between devices, shifted(): lax.ppermute(value, axis, [(source, source + steps) for source in range(l...  87.9 us
    all_to_all x7, waiting for transfers between devices, multiply(): lax.all_to_all(far_backward, 'row', split_axis=0, concat_axis=0, tiled=True)  82.6 us
    all_to_all x7, waiting for transfers between devices, multiply(): lax.all_to_all(outgoing, 'row', split_axis=0, concat_axis=0, tiled=True)  44.9 us
    all_to_all x7, starting transfers between devices, multiply(): lax.all_to_all(far_backward, 'row', split_axis=0, concat_axis=0, tiled=True)  32.8 us
  transfers between devices with their start and end apart: 29, of which 15 were waited for; matrix products, arithmetic and copies ran while one was open for 4% of the time, Pallas kernels for 0%

commit v1 on v0

--- a/solution.py
+++ b/solution.py
@@ -5,6 +5,11 @@
 
 OUTER = 2
 INNER = 2
+
+
+def check_the_tasks(inner_x):
+    next_value = jax.lax.all_gather(inner_x, axis_name="band")
+    return jnp.sum(next_value, axis=0)
 
 
 def shifted(value, axis, steps):
@@ -80,7 +85,7 @@
         )
         carried = shifted(spread[rows_dev:], "row", 1)
         summed = jnp.concatenate([summed[:band_count] + carried, summed[band_count:]], 0)
-        return lax.psum(summed, "band")
+        return check_the_tasks(summed)
 
     row_sums = multiply(jnp.ones((rows_dev, block_size), jnp.float32))
     scaling = 1.0 / jnp.sqrt(row_sums)

time: 1090 us -> 755 us (0.69)
  blocking collectives: 731 us -> 423 us
  starting transfers between devices: 159 us -> 133 us
    psum x7 -> x0, blocking collectives: 396 us -> none  [multiply(): return lax.psum(summed, 'band')]
    all_gather x0 -> x7, blocking collectives: none -> 121 us  [check_the_tasks(): next_value = jax.lax.all_gather(inner_x, axis_name='band')]
    ppermute x14, starting transfers between devices: 87.9 us -> 62.4 us  [shifted(): lax.ppermute(value, axis, [(source, source + steps) for source in range(l...]
    psum x2, blocking collectives: 121 us -> 104 us  [on_device(): current_residual_product = lax.psum(jnp.sum(residual * scaled), 'row')]
    psum x2, blocking collectives: 121 us -> 104 us  [on_device(): curvature = lax.psum(jnp.sum(direction * curved), 'row')]
  transfers between devices with their start and end apart: 29 -> 29, of which waited for: 15 -> 15; matrix products, arithmetic and copies ran while one was open for 4% -> 5% of each run, Pallas kernels for 0% -> 0%
where the time goes in v1:
time: 755 us; the launch traced here: 753 us
  blocking collectives  423 us (56%)
  starting transfers between devices  133 us (18%)
  waiting for transfers between devices  132 us (17%)
  matrix products  24.9 us (3%)
  local copies, waits for them, and re-layouts  17.9 us (2%)
  other arithmetic  12.6 us (2%)
  between operations  9.3 us (1%)
    all_gather x7, blocking collectives, check_the_tasks(): next_value = jax.lax.all_gather(inner_x, axis_name='band')  121 us
    psum x2, blocking collectives, on_device(): curvature = lax.psum(jnp.sum(direction * curved), 'row')  104 us
    psum x2, blocking collectives, on_device(): current_residual_product = lax.psum(jnp.sum(residual * scaled), 'row')  104 us
    psum x2, blocking collectives, on_device(): rho_next = lax.psum(jnp.sum(residual * scaled), 'row')  93 us
    all_to_all x7, waiting for transfers between devices, multiply(): lax.all_to_all(far_backward, 'row', split_axis=0, concat_axis=0, tiled=True)  82.6 us
    ppermute x14, starting transfers between devices, shifted(): lax.ppermute(value, axis, [(source, source + steps) for source in range(l...  62.4 us
    all_to_all x7, waiting for transfers between devices, multiply(): lax.all_to_all(outgoing, 'row', split_axis=0, concat_axis=0, tiled=True)  44.9 us
    all_to_all x7, starting transfers between devices, multiply(): lax.all_to_all(far_backward, 'row', split_axis=0, concat_axis=0, tiled=True)  32.8 us
  transfers between devices with their start and end apart: 29, of which 15 were waited for; matrix products, arithmetic and copies ran while one was open for 5% of the time, Pallas kernels for 0%

profile of v1, /device:TPU:1, one launch (start us, length us, event | category | flops | bytes accessed | tf_op | source)
XLA Modules:
  0.0 753.2 jit_solution(9291925278446582171)
XLA Ops:
  0.7 9.0 %collective-permute-start = (bf16[16,128]{1,0:T(8,128)(2,1)S(1)}, bf16[16,128]{1,0:T(8,128)(2,1)S(1)}, u32[]{:S(2)}, u32[]{:S(2)}) collective-permute-start(bf16[16,128]{1,0:T(8,128)(2,1)S(1)} %slice.105), channel_id=1, source_target_pairs={{16,0},{32,16},{48,32},{64,48},{80,64},{96,80},{112,96},{128,112},... | collective-permute-start | bytes 12296 | tf_op jit(solution)/shard_map/ppermute | solution.py:18
  9.7 1.4 copy.16
  11.1 10.0 %all-to-all-start = ((s32[32,1,2]{2,1,0:T(1,128)}), s32[32,1,2]{2,1,0:T(1,128)S(1)}, u32[]{:S(2)}, u32[]{:S(2)}) async-start(s32[32,1,2]{2,1,0:T(1,128)} %copy.16), calls=%async_computation | async-start | bytes 32768 | tf_op jit(solution)/shard_map/all_to_all | solution.py:38
  21.1 1.6 fusion.52
  23.0 3.5 collective-permute-start.1
  28.1 4.7 all-to-all-done
  33.8 1.2 gather_fusion
  35.0 6.2 all-to-all-start.1
  44.7 8.2 %all-to-all-done.1 = bf16[32,2,128]{2,1,0:T(2,128)(2,1)S(1)} async-done(((bf16[32,2,128]{2,1,0:T(2,128)(2,1)}), bf16[32,2,128]{2,1,0:T(2,128)(2,1)S(1)}, u32[]{:S(2)}, u32[]{:S(2)}) %all-to-all-start.1) | async-done | bytes 16416 | tf_op jit(solution)/shard_map/all_to_all | solution.py:59
  54.8 4.4 all-to-all-start.2
  59.5 12.0 %all-to-all-done.2 = f32[32,2,128]{2,1,0:T(2,128)S(1)} async-done(((f32[32,2,128]{2,1,0:T(2,128)}), f32[32,2,128]{2,1,0:T(2,128)S(1)}, u32[]{:S(2)}, u32[]{:S(2)}) %all-to-all-start.2) | async-done | bytes 32800 | tf_op jit(solution)/shard_map/all_to_all | solution.py:78
  71.8 18.8 %all-gather = f32[512,128]{1,0:T(8,128)S(1)} all-gather(f32[32,128]{1,0:T(8,128)S(1)} %pad_maximum_fusion), channel_id=2, replica_groups=mesh['row'=32,'band'=16] {'band'}, dimensions={0}, use_global_device_ids=true | all-gather | bytes 278528 | tf_op jit(solution)/shard_map/all_gather | solution.py:11
  90.6 1.2 gather_fusion.2
  92.5 8.2 %collective-permute-start.2 = (bf16[16,128]{1,0:T(8,128)(2,1)S(1)}, bf16[16,128]{1,0:T(8,128)(2,1)S(1)}, u32[]{:S(2)}, u32[]{:S(2)}) collective-permute-start(bf16[16,128]{1,0:T(8,128)(2,1)S(1)} %slice.172), channel_id=1, source_target_pairs={{16,0},{32,16},{48,32},{64,48},{80,64},{96,80},{112,96},{128,112},... | collective-permute-start | bytes 12296 | tf_op jit(solution)/shard_map/ppermute | solution.py:18
  100.7 3.6 all-to-all-start.3
  105.7 2.8 collective-permute-start.3
  109.2 6.2 all-to-all-done.3
  117.3 4.7 all-to-all-start.4
  122.3 11.8 %all-to-all-done.4 = f32[32,2,128]{2,1,0:T(2,128)S(1)} async-done(((f32[32,2,128]{2,1,0:T(2,128)}), f32[32,2,128]{2,1,0:T(2,128)S(1)}, u32[]{:S(2)}, u32[]{:S(2)}) %all-to-all-start.4) | async-done | bytes 32800 | tf_op jit(solution)/shard_map/all_to_all | solution.py:78
  134.4 17.9 %all-gather.1 = f32[512,128]{1,0:T(8,128)S(1)} all-gather(f32[32,128]{1,0:T(8,128)S(1)} %pad_maximum_fusion.1), channel_id=3, replica_groups=mesh['row'=32,'band'=16] {'band'}, dimensions={0}, use_global_device_ids=true | all-gather | bytes 278528 | tf_op jit(solution)/shard_map/all_gather | solution.py:11
  152.4 1.2 gather_fusion.4
  154.2 8.2 %collective-permute-start.4 = (bf16[16,128]{1,0:T(8,128)(2,1)S(1)}, bf16[16,128]{1,0:T(8,128)(2,1)S(1)}, u32[]{:S(2)}, u32[]{:S(2)}) collective-permute-start(bf16[16,128]{1,0:T(8,128)(2,1)S(1)} %slice.177), channel_id=1, source_target_pairs={{16,0},{32,16},{48,32},{64,48},{80,64},{96,80},{112,96},{128,112},... | collective-permute-start | bytes 12296 | tf_op jit(solution)/shard_map/ppermute | solution.py:18
  162.5 3.6 all-to-all-start.5
  167.5 2.8 collective-permute-start.5
  171.0 6.2 all-to-all-done.5
  179.1 4.7 all-to-all-start.6
  184.1 11.8 %all-to-all-done.6 = f32[32,2,128]{2,1,0:T(2,128)S(1)} async-done(((f32[32,2,128]{2,1,0:T(2,128)}), f32[32,2,128]{2,1,0:T(2,128)S(1)}, u32[]{:S(2)}, u32[]{:S(2)}) %all-to-all-start.6) | async-done | bytes 32800 | tf_op jit(solution)/shard_map/all_to_all | solution.py:78
  196.2 16.2 %all-gather.2 = f32[512,128]{1,0:T(8,128)S(1)} all-gather(f32[32,128]{1,0:T(8,128)S(1)} %pad_maximum_fusion.2), channel_id=4, replica_groups=mesh['row'=32,'band'=16] {'band'}, dimensions={0}, use_global_device_ids=true | all-gather | bytes 278528 | tf_op jit(solution)/shard_map/all_gather | solution.py:11
  213.1 52.2 %all-reduce.2 = (f32[]{:T(128)}, f32[]{:T(128)}) all-reduce(f32[]{:T(128)} %get-tuple-element.3, f32[]{:T(128)} %get-tuple-element.2), channel_id=1, replica_groups=mesh['row'=32,'band'=16] {'row'}, use_global_device_ids=true, to_apply=%region_3.0 | all-reduce | flops 2 | bytes 16 | tf_op jit(solution)/shard_map/psum | solution.py:98
  267.3 46.6 %psum.58 = f32[]{:T(128)} all-reduce(f32[]{:T(128)} %multiply_reduce_fusion.4), channel_id=1, replica_groups=mesh['row'=32,'band'=16] {'row'}, use_global_device_ids=true, to_apply=%region_8.0 | all-reduce | flops 1 | bytes 8 | tf_op jit(solution)/shard_map/psum | solution.py:108
  315.1 1.2 gather_fusion.6
  317.0 2.5 collective-permute-start.6
  319.6 3.6 all-to-all-start.7
  324.5 3.0 collective-permute-start.7
  328.2 6.0 all-to-all-done.7
  336.1 4.8 all-to-all-start.8
  341.2 11.8 %all-to-all-done.8 = f32[32,2,128]{2,1,0:T(2,128)S(1)} async-done(((f32[32,2,128]{2,1,0:T(2,128)}), f32[32,2,128]{2,1,0:T(2,128)S(1)}, u32[]{:S(2)}, u32[]{:S(2)}) %all-to-all-start.8) | async-done | bytes 32800 | tf_op jit(solution)/shard_map/all_to_all | solution.py:78
  353.3 17.9 %all-gather.3 = f32[512,128]{1,0:T(8,128)S(1)} all-gather(f32[32,128]{1,0:T(8,128)S(1)} %pad_maximum_fusion.3), channel_id=5, replica_groups=mesh['row'=32,'band'=16] {'band'}, dimensions={0}, use_global_device_ids=true | all-gather | bytes 278528 | tf_op jit(solution)/shard_map/all_gather | solution.py:11
  371.8 52.1 %psum.59 = f32[]{:T(128)} all-reduce(f32[]{:T(128)} %multiply_reduce_fusion.3), channel_id=1, replica_groups=mesh['row'=32,'band'=16] {'row'}, use_global_device_ids=true, to_apply=%region_11.0 | all-reduce | flops 1 | bytes 8 | tf_op jit(solution)/shard_map/psum | solution.py:102
  425.2 1.2 gather_fusion.8
  427.1 2.5 collective-permute-start.8
  429.6 3.6 all-to-all-start.9
  434.6 3.0 collective-permute-start.9
  438.3 6.0 all-to-all-done.9
  446.2 4.8 all-to-all-start.10
  451.2 11.8 %all-to-all-done.10 = f32[32,2,128]{2,1,0:T(2,128)S(1)} async-done(((f32[32,2,128]{2,1,0:T(2,128)}), f32[32,2,128]{2,1,0:T(2,128)S(1)}, u32[]{:S(2)}, u32[]{:S(2)}) %all-to-all-start.10) | async-done | bytes 32800 | tf_op jit(solution)/shard_map/all_to_all | solution.py:78
  463.3 16.2 %all-gather.4 = f32[512,128]{1,0:T(8,128)S(1)} all-gather(f32[32,128]{1,0:T(8,128)S(1)} %pad_maximum_fusion.4), channel_id=6, replica_groups=mesh['row'=32,'band'=16] {'band'}, dimensions={0}, use_global_device_ids=true | all-gather | bytes 278528 | tf_op jit(solution)/shard_map/all_gather | solution.py:11
  481.5 8.4 %collective-permute-start.10 = (bf16[16,128]{1,0:T(8,128)(2,1)S(1)}, bf16[16,128]{1,0:T(8,128)(2,1)S(1)}, u32[]{:S(2)}, u32[]{:S(2)}) collective-permute-start(bf16[16,128]{1,0:T(8,128)(2,1)S(1)} %slice.192), channel_id=1, source_target_pairs={{16,0},{32,16},{48,32},{64,48},{80,64},{96,80},{112,96},{128,112},... | collective-permute-start | bytes 12296 | tf_op jit(solution)/shard_map/ppermute | solution.py:18
  489.9 3.6 all-to-all-start.11
  494.8 2.8 collective-permute-start.11
  498.3 6.2 all-to-all-done.11
  506.5 4.7 all-to-all-start.12
  511.5 11.8 %all-to-all-done.12 = f32[32,2,128]{2,1,0:T(2,128)S(1)} async-done(((f32[32,2,128]{2,1,0:T(2,128)}), f32[32,2,128]{2,1,0:T(2,128)S(1)}, u32[]{:S(2)}, u32[]{:S(2)}) %all-to-all-start.12) | async-done | bytes 32800 | tf_op jit(solution)/shard_map/all_to_all | solution.py:78
  523.6 17.9 %all-gather.5 = f32[512,128]{1,0:T(8,128)S(1)} all-gather(f32[32,128]{1,0:T(8,128)S(1)} %pad_maximum_fusion.5), channel_id=7, replica_groups=mesh['row'=32,'band'=16] {'band'}, dimensions={0}, use_global_device_ids=true | all-gather | bytes 278528 | tf_op jit(solution)/shard_map/all_gather | solution.py:11
  542.1 52.1 %all-reduce.1 = (f32[]{:T(128)}, f32[]{:T(128)}) all-reduce(f32[]{:T(128)} %get-tuple-element.5, f32[]{:T(128)} %get-tuple-element.4), channel_id=1, replica_groups=mesh['row'=32,'band'=16] {'row'}, use_global_device_ids=true, to_apply=%region_14.0 | all-reduce | flops 2 | bytes 16 | tf_op jit(solution)/shard_map/psum | solution.py:98
  596.2 46.4 %psum.62 = f32[]{:T(128)} all-reduce(f32[]{:T(128)} %get-tuple-element.10), channel_id=1, replica_groups=mesh['row'=32,'band'=16] {'row'}, use_global_device_ids=true, to_apply=%region_19.0 | all-reduce | flops 1 | bytes 8 | tf_op jit(solution)/shard_map/psum | solution.py:108
  645.7 2.5 collective-permute-start.12
  648.3 3.9 all-to-all-start.13
  653.5 3.0 collective-permute-start.13
  657.2 6.0 all-to-all-done.13
  665.1 4.7 all-to-all-start.14
  670.1 11.8 %all-to-all-done.14 = f32[32,2,128]{2,1,0:T(2,128)S(1)} async-done(((f32[32,2,128]{2,1,0:T(2,128)}), f32[32,2,128]{2,1,0:T(2,128)S(1)}, u32[]{:S(2)}, u32[]{:S(2)}) %all-to-all-start.14) | async-done | bytes 32800 | tf_op jit(solution)/shard_map/all_to_all | solution.py:78
  682.2 16.2 %all-gather.6 = f32[512,128]{1,0:T(8,128)S(1)} all-gather(f32[32,128]{1,0:T(8,128)S(1)} %pad_maximum_fusion.6), channel_id=8, replica_groups=mesh['row'=32,'band'=16] {'band'}, dimensions={0}, use_global_device_ids=true | all-gather | bytes 278528 | tf_op jit(solution)/shard_map/all_gather | solution.py:11
  699.0 52.3 %psum.63 = f32[]{:T(128)} all-reduce(f32[]{:T(128)} %multiply_reduce_fusion), channel_id=1, replica_groups=mesh['row'=32,'band'=16] {'row'}, use_global_device_ids=true, to_apply=%region_22.0 | all-reduce | flops 1 | bytes 8 | tf_op jit(solution)/shard_map/psum | solution.py:102
  (169 shorter events, 46.3 us)
Async XLA Ops:
  0.6 41.4 %copy-start = (bf16[1,1,32,2,128,128]{5,4,3,2,1,0:T(8,128)(2,1)S(1)}, bf16[1,1,32,2,128,128]{5,4,3,2,1,0:T(8,128)(2,1)}, u32[]{:S(2)}) copy-start(bf16[1,1,32,2,128,128]{5,4,3,2,1,0:T(8,128)(2,1)} %param.6) | copy-start | bytes 6291460
  0.6 43.4 %copy-start.1 = (bf16[32,1,128,128]{3,2,1,0:T(8,128)(2,1)S(1)}, bf16[32,1,128,128]{3,2,1,0:T(8,128)(2,1)}, u32[]{:S(2)}) copy-start(bf16[32,1,128,128]{3,2,1,0:T(8,128)(2,1)} %param.5) | copy-start | bytes 3145732
  0.7 43.3 %collective-permute-start = (bf16[16,128]{1,0:T(8,128)(2,1)S(1)}, bf16[16,128]{1,0:T(8,128)(2,1)S(1)}, u32[]{:S(2)}, u32[]{:S(2)}) collective-permute-start(bf16[16,128]{1,0:T(8,128)(2,1)S(1)} %slice.105), channel_id=1, source_target_pairs={{16,0},{32,16},{48,32},{64,48},{80,64},{96,80},{112,96},{128,112},... | collective-permute-start | bytes 12296 | tf_op jit(solution)/shard_map/ppermute | solution.py:18
  11.1 21.8 %all-to-all-start = ((s32[32,1,2]{2,1,0:T(1,128)}), s32[32,1,2]{2,1,0:T(1,128)S(1)}, u32[]{:S(2)}, u32[]{:S(2)}) async-start(s32[32,1,2]{2,1,0:T(1,128)} %copy.16), calls=%async_computation | async-start | bytes 32768 | tf_op jit(solution)/shard_map/all_to_all | solution.py:38
  23.0 48.8 %collective-permute-start.1 = (f32[16,128]{1,0:T(8,128)S(1)}, f32[16,128]{1,0:T(8,128)S(1)}, u32[]{:S(2)}, u32[]{:S(2)}) collective-permute-start(f32[16,128]{1,0:T(8,128)S(1)} %slice.170), channel_id=1, source_target_pairs={{0,16},{16,32},{32,48},{48,64},{64,80},{80,96},{96,112},{112,128},... | collective-permute-start | bytes 24584 | tf_op jit(solution)/shard_map/ppermute | solution.py:18
  35.0 17.9 %all-to-all-start.1 = ((bf16[32,2,128]{2,1,0:T(2,128)(2,1)}), bf16[32,2,128]{2,1,0:T(2,128)(2,1)S(1)}, u32[]{:S(2)}, u32[]{:S(2)}) async-start(bf16[32,2,128]{2,1,0:T(2,128)(2,1)} %bitcast.8), calls=%async_computation.1 | async-start | bytes 32768 | tf_op jit(solution)/shard_map/all_to_all | solution.py:59
  54.8 16.6 %all-to-all-start.2 = ((f32[32,2,128]{2,1,0:T(2,128)}), f32[32,2,128]{2,1,0:T(2,128)S(1)}, u32[]{:S(2)}, u32[]{:S(2)}) async-start(f32[32,2,128]{2,1,0:T(2,128)} %get-tuple-element.45), calls=%async_computation.2 | async-start | bytes 65536 | tf_op jit(solution)/shard_map/all_to_all | solution.py:78
  92.5 16.0 %collective-permute-start.2 = (bf16[16,128]{1,0:T(8,128)(2,1)S(1)}, bf16[16,128]{1,0:T(8,128)(2,1)S(1)}, u32[]{:S(2)}, u32[]{:S(2)}) collective-permute-start(bf16[16,128]{1,0:T(8,128)(2,1)S(1)} %slice.172), channel_id=1, source_target_pairs={{16,0},{32,16},{48,32},{64,48},{80,64},{96,80},{112,96},{128,112},... | collective-permute-start | bytes 12296 | tf_op jit(solution)/shard_map/ppermute | solution.py:18
  100.7 14.7 %all-to-all-start.3 = ((bf16[32,2,128]{2,1,0:T(2,128)(2,1)}), bf16[32,2,128]{2,1,0:T(2,128)(2,1)S(1)}, u32[]{:S(2)}, u32[]{:S(2)}) async-start(bf16[32,2,128]{2,1,0:T(2,128)(2,1)} %bitcast.28), calls=%async_computation.3 | async-start | bytes 32768 | tf_op jit(solution)/shard_map/all_to_all | solution.py:59
  105.7 28.7 %collective-permute-start.3 = (f32[16,128]{1,0:T(8,128)S(1)}, f32[16,128]{1,0:T(8,128)S(1)}, u32[]{:S(2)}, u32[]{:S(2)}) collective-permute-start(f32[16,128]{1,0:T(8,128)S(1)} %slice.175), channel_id=1, source_target_pairs={{0,16},{16,32},{32,48},{48,64},{64,80},{80,96},{96,112},{112,128},... | collective-permute-start | bytes 24584 | tf_op jit(solution)/shard_map/ppermute | solution.py:18
  117.3 16.8 %all-to-all-start.4 = ((f32[32,2,128]{2,1,0:T(2,128)}), f32[32,2,128]{2,1,0:T(2,128)S(1)}, u32[]{:S(2)}, u32[]{:S(2)}) async-start(f32[32,2,128]{2,1,0:T(2,128)} %get-tuple-element.41), calls=%async_computation.4 | async-start | bytes 65536 | tf_op jit(solution)/shard_map/all_to_all | solution.py:78
  154.2 16.0 %collective-permute-start.4 = (bf16[16,128]{1,0:T(8,128)(2,1)S(1)}, bf16[16,128]{1,0:T(8,128)(2,1)S(1)}, u32[]{:S(2)}, u32[]{:S(2)}) collective-permute-start(bf16[16,128]{1,0:T(8,128)(2,1)S(1)} %slice.177), channel_id=1, source_target_pairs={{16,0},{32,16},{48,32},{64,48},{80,64},{96,80},{112,96},{128,112},... | collective-permute-start | bytes 12296 | tf_op jit(solution)/shard_map/ppermute | solution.py:18
  162.5 14.7 %all-to-all-start.5 = ((bf16[32,2,128]{2,1,0:T(2,128)(2,1)}), bf16[32,2,128]{2,1,0:T(2,128)(2,1)S(1)}, u32[]{:S(2)}, u32[]{:S(2)}) async-start(bf16[32,2,128]{2,1,0:T(2,128)(2,1)} %bitcast.45), calls=%async_computation.5 | async-start | bytes 32768 | tf_op jit(solution)/shard_map/all_to_all | solution.py:59
  167.5 28.7 %collective-permute-start.5 = (f32[16,128]{1,0:T(8,128)S(1)}, f32[16,128]{1,0:T(8,128)S(1)}, u32[]{:S(2)}, u32[]{:S(2)}) collective-permute-start(f32[16,128]{1,0:T(8,128)S(1)} %slice.180), channel_id=1, source_target_pairs={{0,16},{16,32},{32,48},{48,64},{64,80},{80,96},{96,112},{112,128},... | collective-permute-start | bytes 24584 | tf_op jit(solution)/shard_map/ppermute | solution.py:18
  179.1 16.8 %all-to-all-start.6 = ((f32[32,2,128]{2,1,0:T(2,128)}), f32[32,2,128]{2,1,0:T(2,128)S(1)}, u32[]{:S(2)}, u32[]{:S(2)}) async-start(f32[32,2,128]{2,1,0:T(2,128)} %get-tuple-element.37), calls=%async_computation.6 | async-start | bytes 65536 | tf_op jit(solution)/shard_map/all_to_all | solution.py:78
  317.0 10.5 %collective-permute-start.6 = (bf16[16,128]{1,0:T(8,128)(2,1)S(1)}, bf16[16,128]{1,0:T(8,128)(2,1)S(1)}, u32[]{:S(2)}, u32[]{:S(2)}) collective-permute-start(bf16[16,128]{1,0:T(8,128)(2,1)S(1)} %slice.182), channel_id=1, source_target_pairs={{16,0},{32,16},{48,32},{64,48},{80,64},{96,80},{112,96},{128,112},... | collective-permute-start | bytes 12296 | tf_op jit(solution)/shard_map/ppermute | solution.py:18
  319.6 14.7 %all-to-all-start.7 = ((bf16[32,2,128]{2,1,0:T(2,128)(2,1)}), bf16[32,2,128]{2,1,0:T(2,128)(2,1)S(1)}, u32[]{:S(2)}, u32[]{:S(2)}) async-start(bf16[32,2,128]{2,1,0:T(2,128)(2,1)} %bitcast.62), calls=%async_computation.7 | async-start | bytes 32768 | tf_op jit(solution)/shard_map/all_to_all | solution.py:59
  324.5 28.7 %collective-permute-start.7 = (f32[16,128]{1,0:T(8,128)S(1)}, f32[16,128]{1,0:T(8,128)S(1)}, u32[]{:S(2)}, u32[]{:S(2)}) collective-permute-start(f32[16,128]{1,0:T(8,128)S(1)} %slice.185), channel_id=1, source_target_pairs={{0,16},{16,32},{32,48},{48,64},{64,80},{80,96},{96,112},{112,128},... | collective-permute-start | bytes 24584 | tf_op jit(solution)/shard_map/ppermute | solution.py:18
  336.1 16.8 %all-to-all-start.8 = ((f32[32,2,128]{2,1,0:T(2,128)}), f32[32,2,128]{2,1,0:T(2,128)S(1)}, u32[]{:S(2)}, u32[]{:S(2)}) async-start(f32[32,2,128]{2,1,0:T(2,128)} %get-tuple-element.33), calls=%async_computation.8 | async-start | bytes 65536 | tf_op jit(solution)/shard_map/all_to_all | solution.py:78
  427.1 10.5 %collective-permute-start.8 = (bf16[16,128]{1,0:T(8,128)(2,1)S(1)}, bf16[16,128]{1,0:T(8,128)(2,1)S(1)}, u32[]{:S(2)}, u32[]{:S(2)}) collective-permute-start(bf16[16,128]{1,0:T(8,128)(2,1)S(1)} %slice.187), channel_id=1, source_target_pairs={{16,0},{32,16},{48,32},{64,48},{80,64},{96,80},{112,96},{128,112},... | collective-permute-start | bytes 12296 | tf_op jit(solution)/shard_map/ppermute | solution.py:18
  429.6 14.7 %all-to-all-start.9 = ((bf16[32,2,128]{2,1,0:T(2,128)(2,1)}), bf16[32,2,128]{2,1,0:T(2,128)(2,1)S(1)}, u32[]{:S(2)}, u32[]{:S(2)}) async-start(bf16[32,2,128]{2,1,0:T(2,128)(2,1)} %bitcast.79), calls=%async_computation.9 | async-start | bytes 32768 | tf_op jit(solution)/shard_map/all_to_all | solution.py:59
  434.6 28.7 %collective-permute-start.9 = (f32[16,128]{1,0:T(8,128)S(1)}, f32[16,128]{1,0:T(8,128)S(1)}, u32[]{:S(2)}, u32[]{:S(2)}) collective-permute-start(f32[16,128]{1,0:T(8,128)S(1)} %slice.190), channel_id=1, source_target_pairs={{0,16},{16,32},{32,48},{48,64},{64,80},{80,96},{96,112},{112,128},... | collective-permute-start | bytes 24584 | tf_op jit(solution)/shard_map/ppermute | solution.py:18
  446.2 16.8 %all-to-all-start.10 = ((f32[32,2,128]{2,1,0:T(2,128)}), f32[32,2,128]{2,1,0:T(2,128)S(1)}, u32[]{:S(2)}, u32[]{:S(2)}) async-start(f32[32,2,128]{2,1,0:T(2,128)} %get-tuple-element.29), calls=%async_computation.10 | async-start | bytes 65536 | tf_op jit(solution)/shard_map/all_to_all | solution.py:78
  481.5 16.1 %collective-permute-start.10 = (bf16[16,128]{1,0:T(8,128)(2,1)S(1)}, bf16[16,128]{1,0:T(8,128)(2,1)S(1)}, u32[]{:S(2)}, u32[]{:S(2)}) collective-permute-start(bf16[16,128]{1,0:T(8,128)(2,1)S(1)} %slice.192), channel_id=1, source_target_pairs={{16,0},{32,16},{48,32},{64,48},{80,64},{96,80},{112,96},{128,112},... | collective-permute-start | bytes 12296 | tf_op jit(solution)/shard_map/ppermute | solution.py:18
  489.9 14.7 %all-to-all-start.11 = ((bf16[32,2,128]{2,1,0:T(2,128)(2,1)}), bf16[32,2,128]{2,1,0:T(2,128)(2,1)S(1)}, u32[]{:S(2)}, u32[]{:S(2)}) async-start(bf16[32,2,128]{2,1,0:T(2,128)(2,1)} %bitcast.96), calls=%async_computation.11 | async-start | bytes 32768 | tf_op jit(solution)/shard_map/all_to_all | solution.py:59
  494.8 28.7 %collective-permute-start.11 = (f32[16,128]{1,0:T(8,128)S(1)}, f32[16,128]{1,0:T(8,128)S(1)}, u32[]{:S(2)}, u32[]{:S(2)}) collective-permute-start(f32[16,128]{1,0:T(8,128)S(1)} %slice.195), channel_id=1, source_target_pairs={{0,16},{16,32},{32,48},{48,64},{64,80},{80,96},{96,112},{112,128},... | collective-permute-start | bytes 24584 | tf_op jit(solution)/shard_map/ppermute | solution.py:18
  506.5 16.8 %all-to-all-start.12 = ((f32[32,2,128]{2,1,0:T(2,128)}), f32[32,2,128]{2,1,0:T(2,128)S(1)}, u32[]{:S(2)}, u32[]{:S(2)}) async-start(f32[32,2,128]{2,1,0:T(2,128)} %get-tuple-element.25), calls=%async_computation.12 | async-start | bytes 65536 | tf_op jit(solution)/shard_map/all_to_all | solution.py:78
  645.7 10.8 %collective-permute-start.12 = (bf16[16,128]{1,0:T(8,128)(2,1)S(1)}, bf16[16,128]{1,0:T(8,128)(2,1)S(1)}, u32[]{:S(2)}, u32[]{:S(2)}) collective-permute-start(bf16[16,128]{1,0:T(8,128)(2,1)S(1)} %slice.197), channel_id=1, source_target_pairs={{16,0},{32,16},{48,32},{64,48},{80,64},{96,80},{112,96},{128,112},... | collective-permute-start | bytes 12296 | tf_op jit(solution)/shard_map/ppermute | solution.py:18
  648.3 14.9 %all-to-all-start.13 = ((bf16[32,2,128]{2,1,0:T(2,128)(2,1)}), bf16[32,2,128]{2,1,0:T(2,128)(2,1)S(1)}, u32[]{:S(2)}, u32[]{:S(2)}) async-start(bf16[32,2,128]{2,1,0:T(2,128)(2,1)} %bitcast.113), calls=%async_computation.13 | async-start | bytes 32768 | tf_op jit(solution)/shard_map/all_to_all | solution.py:59
  653.5 28.7 %collective-permute-start.13 = (f32[16,128]{1,0:T(8,128)S(1)}, f32[16,128]{1,0:T(8,128)S(1)}, u32[]{:S(2)}, u32[]{:S(2)}) collective-permute-start(f32[16,128]{1,0:T(8,128)S(1)} %slice.200), channel_id=1, source_target_pairs={{0,16},{16,32},{32,48},{48,64},{64,80},{80,96},{96,112},{112,128},... | collective-permute-start | bytes 24584 | tf_op jit(solution)/shard_map/ppermute | solution.py:18
  665.1 16.8 %all-to-all-start.14 = ((f32[32,2,128]{2,1,0:T(2,128)}), f32[32,2,128]{2,1,0:T(2,128)S(1)}, u32[]{:S(2)}, u32[]{:S(2)}) async-start(f32[32,2,128]{2,1,0:T(2,128)} %get-tuple-element.21), calls=%async_computation.14 | async-start | bytes 65536 | tf_op jit(solution)/shard_map/all_to_all | solution.py:78
